TPU v7x, 32 devices: a whole 2x2x4 slice. The times are simulated.
32 devices in a mesh: shard: 4 (over z), rep: 8 (over y, x, core).
Axes of the slice: x: 2, y: 2, z: 4, core: 2. Of those that a mesh axis runs over, the one named last changes fastest.
Arguments:
- grads: bfloat16 [1, 8192, 28672], P(None, 'shard', 'rep'), may hold values from -81 to 81
- seeds: int32 [1], replicated, may hold values from 0 to 999999
Outputs:
- projected: bfloat16 [512, 1, 28672], P('shard', None, 'rep')
All inputs are finite; a program needn't handle non-finite values.
Results may differ from a plain program's by a relative error of at most 0.0056.
Values may be sent and summed in bfloat16 or wider, within the bound.
No kernel may reach another device: no remote copies, remote signals or barrier semaphores. Data moves between devices by JAX's collectives and lax.ppermute only.
A program may use at most 128 MiB of HBM per device.

v0:
```python
import jax
import jax.numpy as jnp
from jax import lax
from jax.sharding import PartitionSpec as P

RANK = 512
mix_first = 668265263
mix_second = -2048144789
mix_third = -1028477387


def sketch_table(seeds, first_row, count, rank):
    rows = first_row + lax.iota(jnp.int32, count)
    columns = lax.iota(jnp.int32, rank)
    counter = rows[:, None] * jnp.int32(rank) + columns[None, :]
    hashed = jnp.bitwise_xor(counter[None, :, :], (seeds * jnp.int32(mix_first))[:, None, None])
    hashed = hashed * jnp.int32(mix_second)
    hashed = jnp.bitwise_xor(hashed, lax.shift_right_logical(hashed, jnp.int32(15)))
    hashed = hashed * jnp.int32(mix_third)
    hashed = jnp.bitwise_xor(hashed, lax.shift_right_logical(hashed, jnp.int32(13)))
    unit = lax.shift_right_logical(hashed, jnp.int32(8)).astype(jnp.float32) * (1.0 / 16777216.0)
    return (2.0 * unit - 1.0).astype(jnp.bfloat16)


def body(grads, seeds):
    mats, depth, width = grads.shape
    rows_whole = lax.all_to_all(grads, "rep", split_axis=1, concat_axis=2, tiled=True)
    block = rows_whole.shape[2] // 8

    def add_block(step, total):
        start = step * block
        table = sketch_table(seeds, start, block, RANK)
        piece = lax.dynamic_slice_in_dim(rows_whole, start, block, 2)
        return total + jnp.einsum("mdc,mcr->dmr", piece, table, preferred_element_type=jnp.float32)

    sketch_rows = lax.fori_loop(
        0, 8, add_block, jnp.zeros((rows_whole.shape[1], mats, RANK), jnp.float32)
    )
    local_gram = jnp.einsum(
        "dmr,dms->mrs",
        sketch_rows,
        sketch_rows,
        precision=lax.Precision.HIGHEST,
        preferred_element_type=jnp.float32,
    )
    gram = lax.psum(local_gram, ("shard", "rep"))
    factor = jnp.linalg.cholesky(gram)
    own_rows = jnp.transpose(sketch_rows, (1, 0, 2))
    basis_rows = lax.linalg.triangular_solve(
        factor, own_rows, left_side=False, lower=True, transpose_a=True
    ).astype(jnp.bfloat16)
    partial_sum = jnp.einsum(
        "mdr,mdc->rmc",
        lax.all_gather(basis_rows, "rep", axis=1, tiled=True),
        grads,
        preferred_element_type=jnp.float32,
    )
    projected = lax.psum_scatter(partial_sum, "shard", scatter_dimension=0, tiled=True)
    return projected.astype(jnp.bfloat16)


def solution(mesh):
    return jax.shard_map(
        body,
        mesh=mesh,
        in_specs=(P(None, "shard", "rep"), P()),
        out_specs=P("shard", None, "rep"),
        check_vma=False,
    )
```

profile of v0, /device:TPU:0, one launch (start us, length us, event | category | flops | bytes accessed | tf_op | source)
XLA Modules:
  0.0 861.6 jit_solution(14677463218900408071)
XLA Ops:
  6.5 26.0 %copy.30 = bf16[1,2048,3584]{2,0,1:T(2,128)(2,1)} copy(bf16[1,2048,3584]{2,1,0:T(8,128)(2,1)} %param.4) | data formatting | bytes 29360128 | tf_op args[0]
  33.1 94.1 %reduce.36 = bf16[2048,3584]{1,0:T(8,128)(2,1)} reduce(bf16[2048,1,3584]{2,1,0:T(2,128)(2,1)} %bitcast.210, bf16[]{:T(256)} %broadcast.502), dimensions={1}, to_apply=%bitcast.195.reduce_sub_computation | reduce | bytes 29360130
  127.2 16.3 %reshape.459 = bf16[8,2,458752]{2,1,0:T(2,128)(2,1)} reshape(bf16[2048,3584]{1,0:T(8,128)(2,1)} %reduce.36) | data formatting | bytes 29360128
  143.5 5.6 all-to-all-start
  149.9 161.3 %all-to-all-done = bf16[8,2,458752]{2,1,0:T(2,128)(2,1)} async-done(((bf16[8,2,458752]{2,1,0:T(2,128)(2,1)}), bf16[8,2,458752]{2,1,0:T(2,128)(2,1)}, u32[]{:S(2)}, u32[]{:S(2)}) %all-to-all-start) | async-done | bytes 14680096 | tf_op jit(solution)/shard_map/all_to_all | solution.py:27
  311.2 20.2 %reshape.460 = bf16[2048,1,3584]{2,1,0:T(2,128)(2,1)} reshape(bf16[8,2,458752]{2,1,0:T(2,128)(2,1)} %all-to-all-done) | data formatting | bytes 29360128
  331.4 19.4 %copy.28 = bf16[1,2048,3584]{2,1,0:T(8,128)(2,1)} copy(bf16[1,2048,3584]{2,0,1:T(2,128)(2,1)} %bitcast.211) | data formatting | bytes 29360128
  350.8 18.7 %copy.21 = bf16[1,256,8,3584]{1,3,2,0:T(8,128)(2,1)} copy(bf16[1,256,8,3584]{3,1,2,0:T(8,128)(2,1)} %bitcast.212) | data formatting | bytes 29360128 | tf_op jit(solution)/shard_map/all_to_all | solution.py:27
  369.5 42.8 %while.18 = (s32[]{:T(128)}, f32[256,1,512]{0,2,1:T(8,128)S(1)}, s32[1]{0:T(128)}, bf16[1,256,28672]{1,2,0:T(8,128)(2,1)}, s32[]{:T(128)}, /*index=5*/s32[]{:T(128)}, s32[]{:T(128)}, s32[]{:T(128)}) while((s32[]{:T(128)}, f32[256,1,512]{0,2,1:T(8,128)S(1)}, s32[1]{0:T(128)}, bf16[1,256,28672]{1,2,0:T(8,128)(2,1)}, s32[]{:T(128)}, ...), condition=%wide.region_1.0_spmd.clone, body=%wide.region_0.0_spmd.clone.sunk | while | flops 963648512 | bytes 2912917 | solution.py:36
  369.5 5.3 fusion.77
  374.8 5.3 fusion.77
  380.2 5.3 fusion.77
  385.5 5.3 fusion.77
  390.9 5.3 fusion.77
  396.2 5.3 fusion.77
  401.6 5.3 fusion.77
  407.0 5.3 fusion.77
  412.3 2.1 convolution_bitcast_fusion
  414.9 130.6 %all-reduce.3.cloned.1.call-done = f32[1,512,512]{1,2,0:T(8,128)} async-done(((f32[1,512,512]{1,2,0:T(8,128)}), f32[1,512,512]{1,2,0:T(8,128)}) %all-reduce.3.cloned.1.call-update) | async-done | bytes 1048592 | tf_op jit(solution)/shard_map/psum | solution.py:46
  545.5 1.6 copy.25
  547.1 1.4 fusion.47
  548.5 11.7 %custom-call.34 = f32[1,128,128]{2,1,0:T(8,128)S(1)} custom-call(f32[1,128,128]{2,1,0:T(8,128)S(1)} %cholesky.267), custom_call_target="Cholesky" | custom-call | tf_op jit(solution)/shard_map/jit(cholesky)/cholesky | solution.py:47
  560.3 9.8 %custom-call.35 = f32[1,1,128,128]{2,3,1,0:T(8,128)S(1)} custom-call(f32[1,1,128,128]{3,2,1,0:T(8,128)S(1)} %get-tuple-element.173), custom_call_target="InvertDiagBlocksLowerTriangular" | custom-call | tf_op jit(solution)/shard_map/jit(cholesky)/cholesky | solution.py:47
  570.9 11.7 %custom-call.36 = f32[1,128,128]{2,1,0:T(8,128)S(1)} custom-call(f32[1,128,128]{2,1,0:T(8,128)S(1)} %cholesky.271), custom_call_target="Cholesky" | custom-call | tf_op jit(solution)/shard_map/jit(cholesky)/cholesky | solution.py:47
  582.6 10.2 %custom-call.37 = f32[1,1,128,128]{2,3,1,0:T(8,128)S(1)} custom-call(f32[1,1,128,128]{3,2,1,0:T(8,128)S(1)} %get-tuple-element.170), custom_call_target="InvertDiagBlocksLowerTriangular" | custom-call | tf_op jit(solution)/shard_map/jit(cholesky)/cholesky | solution.py:47
  593.5 11.7 %custom-call.38 = f32[1,128,128]{2,1,0:T(8,128)S(1)} custom-call(f32[1,128,128]{2,1,0:T(8,128)S(1)} %cholesky.276), custom_call_target="Cholesky" | custom-call | tf_op jit(solution)/shard_map/jit(cholesky)/cholesky | solution.py:47
  605.2 0.7 compare_reduce_fusion.1
  606.0 9.8 %custom-call.39 = f32[1,1,128,128]{2,3,1,0:T(8,128)S(1)} custom-call(f32[1,1,128,128]{3,2,1,0:T(8,128)S(1)} %get-tuple-element.167), custom_call_target="InvertDiagBlocksLowerTriangular" | custom-call | tf_op jit(solution)/shard_map/jit(cholesky)/cholesky | solution.py:47
  616.4 11.7 %custom-call.40 = f32[1,128,128]{2,1,0:T(8,128)S(1)} custom-call(f32[1,128,128]{2,1,0:T(8,128)S(1)} %fusion.46), custom_call_target="Cholesky" | custom-call | tf_op jit(solution)/shard_map/jit(cholesky)/cholesky | solution.py:47
  628.1 0.6 compare_reduce_fusion
  628.8 0.9 compare_reduce_fusion.2
  632.3 8.1 while.17
  632.4 0.6 fusion.74
  633.0 1.3 bitcast_dynamic-update-slice_fusion.2
  634.4 0.6 fusion.74
  635.0 1.3 bitcast_dynamic-update-slice_fusion.2
  636.5 0.6 fusion.74
  637.1 1.3 bitcast_dynamic-update-slice_fusion.2
  638.5 0.6 fusion.74
  639.1 1.3 bitcast_dynamic-update-slice_fusion.2
  640.4 39.3 %custom-call.41 = f32[1,4,128,128]{2,3,1,0:T(8,128)S(1)} custom-call(f32[1,4,128,128]{3,2,1,0:T(8,128)S(1)} %bitcast.221), custom_call_target="InvertDiagBlocksLowerTriangular" | custom-call | tf_op jit(solution)/shard_map/triangular_solve | solution.py:49
  680.8 0.6 fusion.41
  681.7 0.8 fusion.43
  682.9 0.7 pad_maximum_fusion
  683.7 27.2 %all-gather.2.cloned.1.call-done = bf16[1,2048,512]{1,2,0:T(8,128)(2,1)} async-done(((bf16[1,256,512]{1,2,0:T(8,128)(2,1)}), bf16[1,2048,512]{1,2,0:T(8,128)(2,1)}) %all-gather.2.cloned.1.call-update) | async-done | bytes 2097168 | tf_op jit(solution)/shard_map/all_gather | solution.py:54
  710.9 13.5 %fusion.31 = f32[512,1,3584]{2,0,1:T(8,128)} fusion(bf16[1,2048,3584]{2,1,0:T(8,128)(2,1)} %param.4, bf16[1,2048,512]{1,2,0:T(8,128)(2,1)} %all-gather.2.cloned.1.call-done), kind=kOutput, calls=%fused_computation.27 | convolution fusion | flops 7516192768 | bytes 24117248 | tf_op jit(solution)/shard_map/mdr,mdc->rmc/dot_general | solution.py:52
  724.4 127.9 %reduce-scatter.2.cloned.1.call-done = f32[128,1,3584]{2,0,1:T(8,128)} async-done(((f32[512,1,3584]{2,0,1:T(8,128)}), f32[128,1,3584]{2,0,1:T(8,128)}) %reduce-scatter.2.cloned.1.call-update) | async-done | bytes 1835024 | tf_op jit(solution)/shard_map/reduce_scatter | solution.py:58
  852.3 2.5 convert_element_type.66
  (44 shorter events, 5.6 us)
Async XLA Ops:
  143.5 167.7 %all-to-all-start = ((bf16[8,2,458752]{2,1,0:T(2,128)(2,1)}), bf16[8,2,458752]{2,1,0:T(2,128)(2,1)}, u32[]{:S(2)}, u32[]{:S(2)}) async-start(bf16[8,2,458752]{2,1,0:T(2,128)(2,1)} %reshape.459), calls=%async_computation | async-start | bytes 29360128 | tf_op jit(solution)/shard_map/all_to_all | solution.py:27
  149.1 396.4 %all-reduce.3.cloned.1.call-start = ((), (), s32[]{:S(2)}) async-start(), calls=%async_computation.2 | async-start | bytes 2097152 | tf_op jit(solution)/shard_map/psum | solution.py:46
  414.4 296.5 %all-gather.2.cloned.1.call-start = ((), (), s32[]{:S(2)}) async-start(), calls=%async_computation.3 | async-start | bytes 2359296 | tf_op jit(solution)/shard_map/all_gather | solution.py:54
  683.6 168.7 %reduce-scatter.2.cloned.1.call-start = ((), (), s32[]{:S(2)}) async-start(), calls=%async_computation.4 | async-start | bytes 9175040 | tf_op jit(solution)/shard_map/reduce_scatter | solution.py:58
Sparse Core Ops, SparseCore 0:
  414.5 130.9 all-reduce.2
  683.8 27.0 all-gather.1
  724.5 127.7 reduce-scatter.1
where the time goes:
time: 869 us; the launch traced here: 862 us
  waiting for transfers between devices  447 us (51%)
  other arithmetic  217 us (25%)
  local copies, waits for them, and re-layouts  111 us (13%)
  matrix products  63 us (7%)
  between operations  16.7 us (2%)
    all_to_all x1, waiting for transfers between devices, body(): lax.all_to_all(grads, 'rep', split_axis=1, concat_axis=2, tiled=True)  161 us
    psum x1, waiting for transfers between devices, body(): gram = lax.psum(local_gram, ('shard', 'rep'))  131 us
    reduce_scatter x1, waiting for transfers between devices, body(): lax.psum_scatter(partial_sum, 'shard', scatter_dimension=0, tiled=True)  128 us
    unnamed x3, other arithmetic  94.1 us
    unnamed x5, local copies, waits for them, and re-layouts  82.4 us
    another operation x14, other arithmetic, body(): factor = jnp.linalg.cholesky(gram)  79 us
    dot_general x8, matrix products, add_block(): jnp.einsum('mdc,mcr->dmr', piece, table, preferred_element_type=jnp.float32)  42.5 us
    another operation x4, other arithmetic, body(): lax.linalg.triangular_solve(factor, own_rows, left_side=False, lower=True...  40.2 us
  transfers between devices with their start and end apart: 4, of which 4 were waited for; matrix products, arithmetic and copies ran while one was open for 0% of the time, Pallas kernels for 0%

commit v1 on v0

--- a/solution.py
+++ b/solution.py
@@ -2,6 +2,7 @@
 import jax.numpy as jnp
 from jax import lax
 from jax.sharding import PartitionSpec as P
+from jax.lax import axis_index, axis_size, ppermute
 
 RANK = 512
 mix_first = 668265263
@@ -49,12 +50,23 @@
     basis_rows = lax.linalg.triangular_solve(
         factor, own_rows, left_side=False, lower=True, transpose_a=True
     ).astype(jnp.bfloat16)
-    partial_sum = jnp.einsum(
-        "mdr,mdc->rmc",
-        lax.all_gather(basis_rows, "rep", axis=1, tiled=True),
-        grads,
-        preferred_element_type=jnp.float32,
-    )
+    small = axis_size("rep")
+    t1 = axis_index("rep")
+    v_now, heard, part_now = (small, t1, basis_rows.shape[1])
+    block_list = [(dev_j, (dev_j + 1) % v_now) for dev_j in range(v_now)]
+    arr_now, partial_sum = (basis_rows, None)
+    for no in range(v_now):
+        upper = ppermute(arr_now, "rep", perm=block_list) if no < v_now - 1 else None
+        before = jnp.einsum(
+            "mdr,mdc->rmc",
+            arr_now,
+            lax.dynamic_slice_in_dim(
+                grads, (heard - no) % v_now * part_now, arr_now.shape[1], axis=1
+            ),
+            preferred_element_type=jnp.float32,
+        )
+        partial_sum = before if partial_sum is None else partial_sum + before
+        arr_now = upper
     projected = lax.psum_scatter(partial_sum, "shard", scatter_dimension=0, tiled=True)
     return projected.astype(jnp.bfloat16)
 

time: 869 us -> 902 us (1.038)
  matrix products: 63 us -> 106 us
  waiting for transfers between devices: 447 us -> 431 us
    dot_general x1 -> x8, matrix products: 13.5 us -> 53.3 us  [body(): jnp.einsum('mdr,mdc->rmc', arr_now, lax.dynamic_slice_in_dim(grads, (hear...]
    all_gather x1 -> x0, waiting for transfers between devices: 27.2 us -> none  [body(): lax.all_gather(basis_rows, 'rep', axis=1, tiled=True)]
    ppermute x0 -> x7, waiting for transfers between devices: none -> 13.8 us  [body(): ppermute(arr_now, 'rep', perm=block_list)]
    unnamed x5 -> x13, local copies, waits for them, and re-layouts: 82.4 us -> 82.5 us
    unnamed x3 -> x4, other arithmetic: 94.1 us -> 94.1 us
  transfers between devices with their start and end apart: 4 -> 10, of which waited for: 4 -> 10; matrix products, arithmetic and copies ran while one was open for 0% -> 4% of each run, Pallas kernels for 0% -> 0%
where the time goes in v1:
time: 902 us; the launch traced here: 894 us
  waiting for transfers between devices  431 us (48%)
  other arithmetic  216 us (24%)
  local copies, waits for them, and re-layouts  116 us (13%)
  matrix products  106 us (12%)
  between operations  17.2 us (2%)
    all_to_all x1, waiting for transfers between devices, body(): lax.all_to_all(grads, 'rep', split_axis=1, concat_axis=2, tiled=True)  161 us
    psum x1, waiting for transfers between devices, body(): gram = lax.psum(local_gram, ('shard', 'rep'))  130 us
    reduce_scatter x1, waiting for transfers between devices, body(): lax.psum_scatter(partial_sum, 'shard', scatter_dimension=0, tiled=True)  127 us
    unnamed x4, other arithmetic  94.1 us
    unnamed x13, local copies, waits for them, and re-layouts  82.5 us
    another operation x14, other arithmetic, body(): factor = jnp.linalg.cholesky(gram)  78.9 us
    dot_general x8, matrix products, body(): jnp.einsum('mdr,mdc->rmc', arr_now, lax.dynamic_slice_in_dim(grads, (hear...  53.3 us
    dot_general x8, matrix products, add_block(): jnp.einsum('mdc,mcr->dmr', piece, table, preferred_element_type=jnp.float32)  42.5 us
  transfers between devices with their start and end apart: 10, of which 10 were waited for; matrix products, arithmetic and copies ran while one was open for 4% of the time, Pallas kernels for 0%

profile of v1, /device:TPU:0, one launch (start us, length us, event | category | flops | bytes accessed | tf_op | source)
XLA Modules:
  0.0 894.3 jit_solution(12096489681459545140)
XLA Ops:
  6.5 26.0 %copy.35 = bf16[1,2048,3584]{2,0,1:T(2,128)(2,1)} copy(bf16[1,2048,3584]{2,1,0:T(8,128)(2,1)} %param.4) | data formatting | bytes 29360128 | tf_op args[0]
  33.1 94.1 %reduce.36 = bf16[2048,3584]{1,0:T(8,128)(2,1)} reduce(bf16[2048,1,3584]{2,1,0:T(2,128)(2,1)} %bitcast.244, bf16[]{:T(256)} %broadcast.510), dimensions={1}, to_apply=%bitcast.229.reduce_sub_computation | reduce | bytes 29360130
  127.2 16.2 %reshape.534 = bf16[8,2,458752]{2,1,0:T(2,128)(2,1)} reshape(bf16[2048,3584]{1,0:T(8,128)(2,1)} %reduce.36) | data formatting | bytes 29360128
  143.5 5.6 all-to-all-start
  149.9 161.3 %all-to-all-done = bf16[8,2,458752]{2,1,0:T(2,128)(2,1)} async-done(((bf16[8,2,458752]{2,1,0:T(2,128)(2,1)}), bf16[8,2,458752]{2,1,0:T(2,128)(2,1)}, u32[]{:S(2)}, u32[]{:S(2)}) %all-to-all-start) | async-done | bytes 14680096 | tf_op jit(solution)/shard_map/all_to_all | solution.py:28
  311.2 20.2 %reshape.535 = bf16[2048,1,3584]{2,1,0:T(2,128)(2,1)} reshape(bf16[8,2,458752]{2,1,0:T(2,128)(2,1)} %all-to-all-done) | data formatting | bytes 29360128
  331.4 19.4 %copy.33 = bf16[1,2048,3584]{2,1,0:T(8,128)(2,1)} copy(bf16[1,2048,3584]{2,0,1:T(2,128)(2,1)} %bitcast.245) | data formatting | bytes 29360128
  350.8 18.7 %copy.25 = bf16[1,256,8,3584]{1,3,2,0:T(8,128)(2,1)} copy(bf16[1,256,8,3584]{3,1,2,0:T(8,128)(2,1)} %bitcast.246) | data formatting | bytes 29360128 | tf_op jit(solution)/shard_map/all_to_all | solution.py:28
  369.5 42.8 %while.18 = (s32[]{:T(128)}, f32[256,1,512]{0,2,1:T(8,128)S(1)}, s32[1]{0:T(128)}, bf16[1,256,28672]{1,2,0:T(8,128)(2,1)}, s32[]{:T(128)}, /*index=5*/s32[]{:T(128)}, s32[]{:T(128)}, s32[]{:T(128)}) while((s32[]{:T(128)}, f32[256,1,512]{0,2,1:T(8,128)S(1)}, s32[1]{0:T(128)}, bf16[1,256,28672]{1,2,0:T(8,128)(2,1)}, s32[]{:T(128)}, ...), condition=%wide.region_1.0_spmd.clone, body=%wide.region_0.0_spmd.clone.sunk | while | flops 963648512 | bytes 2912925 | solution.py:37
  369.5 5.3 fusion.119
  374.8 5.3 fusion.119
  380.2 5.3 fusion.119
  385.6 5.3 fusion.119
  390.9 5.3 fusion.119
  396.3 5.3 fusion.119
  401.6 5.3 fusion.119
  407.0 5.3 fusion.119
  412.3 2.1 convolution_bitcast_fusion
  415.9 129.5 %all-reduce.3.cloned.1.call-done = f32[1,512,512]{1,2,0:T(8,128)} async-done(((f32[1,512,512]{1,2,0:T(8,128)}), f32[1,512,512]{1,2,0:T(8,128)}) %all-reduce.3.cloned.1.call-update) | async-done | bytes 1048592 | tf_op jit(solution)/shard_map/psum | solution.py:47
  548.4 11.7 %custom-call.34 = f32[1,128,128]{2,1,0:T(8,128)S(1)} custom-call(f32[1,128,128]{2,1,0:T(8,128)S(1)} %cholesky.267), custom_call_target="Cholesky" | custom-call | tf_op jit(solution)/shard_map/jit(cholesky)/cholesky | solution.py:48
  560.2 9.8 %custom-call.35 = f32[1,1,128,128]{2,3,1,0:T(8,128)S(1)} custom-call(f32[1,1,128,128]{3,2,1,0:T(8,128)S(1)} %get-tuple-element.179), custom_call_target="InvertDiagBlocksLowerTriangular" | custom-call | tf_op jit(solution)/shard_map/jit(cholesky)/cholesky | solution.py:48
  570.8 11.7 %custom-call.36 = f32[1,128,128]{2,1,0:T(8,128)S(1)} custom-call(f32[1,128,128]{2,1,0:T(8,128)S(1)} %cholesky.271), custom_call_target="Cholesky" | custom-call | tf_op jit(solution)/shard_map/jit(cholesky)/cholesky | solution.py:48
  582.5 10.2 %custom-call.37 = f32[1,1,128,128]{2,3,1,0:T(8,128)S(1)} custom-call(f32[1,1,128,128]{3,2,1,0:T(8,128)S(1)} %get-tuple-element.176), custom_call_target="InvertDiagBlocksLowerTriangular" | custom-call | tf_op jit(solution)/shard_map/jit(cholesky)/cholesky | solution.py:48
  593.4 11.7 %custom-call.38 = f32[1,128,128]{2,1,0:T(8,128)S(1)} custom-call(f32[1,128,128]{2,1,0:T(8,128)S(1)} %cholesky.276), custom_call_target="Cholesky" | custom-call | tf_op jit(solution)/shard_map/jit(cholesky)/cholesky | solution.py:48
  605.9 9.8 %custom-call.39 = f32[1,1,128,128]{2,3,1,0:T(8,128)S(1)} custom-call(f32[1,1,128,128]{3,2,1,0:T(8,128)S(1)} %get-tuple-element.173), custom_call_target="InvertDiagBlocksLowerTriangular" | custom-call | tf_op jit(solution)/shard_map/jit(cholesky)/cholesky | solution.py:48
  616.3 11.8 %custom-call.40 = f32[1,128,128]{2,1,0:T(8,128)S(1)} custom-call(f32[1,128,128]{2,1,0:T(8,128)S(1)} %fusion.62), custom_call_target="Cholesky" | custom-call | tf_op jit(solution)/shard_map/jit(cholesky)/cholesky | solution.py:48
  632.0 10.5 %while.17 = (s32[]{:T(128)}, f32[1,512,512]{2,1,0:T(8,128)S(1)}, s32[4,2]{0,1:T(2,128)S(1)}, f32[4,1,128,128]{3,2,1,0:T(8,128)}, s32[]{:T(128)}) while((s32[]{:T(128)}, f32[1,512,512]{2,1,0:T(8,128)S(1)}, s32[4,2]{0,1:T(2,128)S(1)}, f32[4,1,128,128]{3,2,1,0:T(8,128)}, s32[]{:T(128)}) %tuple.72), condition=%wide.while_cond, body=%wide.while_body.sunk | while | flops 2 | bytes 132205 | solution.py:50
  632.7 2.0 bitcast_dynamic-update-slice_fusion.2
  635.3 2.0 bitcast_dynamic-update-slice_fusion.2
  637.9 2.0 bitcast_dynamic-update-slice_fusion.2
  640.5 2.0 bitcast_dynamic-update-slice_fusion.2
  642.5 40.1 %custom-call.41 = f32[1,4,128,128]{2,3,1,0:T(8,128)S(1)} custom-call(f32[1,4,128,128]{3,2,1,0:T(8,128)} %bitcast.261), custom_call_target="InvertDiagBlocksLowerTriangular" | custom-call | tf_op jit(solution)/shard_map/triangular_solve | solution.py:50
  687.3 1.7 fusion.60
  689.5 5.8 fusion.42
  696.8 5.7 fusion.40
  702.9 4.2 fusion.38
  707.0 2.5 collective-permute-done.2
  709.5 4.1 fusion.36
  713.6 2.6 collective-permute-done.3
  716.2 4.2 fusion.34
  720.4 2.5 collective-permute-done.4
  723.1 4.1 fusion.32
  727.3 2.5 collective-permute-done.5
  729.8 4.2 fusion.30
  734.0 2.5 collective-permute-done.6
  736.5 21.0 %add_bitcast_fusion = f32[512,1,3584]{0,2,1:T(8,128)} fusion(f32[3584,512]{1,0:T(8,128)} %fusion.30, f32[3584,512]{1,0:T(8,128)} %fusion.32, f32[3584,512]{1,0:T(8,128)} %fusion.34, f32[3584,512]{1,0:T(8,128)} %fusion.36, f32[3584,512]{1,0:T(8,128)} %fusion.38, f32[3584,512]{1,0:T(8,128)} %fusion.42, f32[3584,512]{1,0:T(8,128)} %fusion.40, ...), kind=kOutput, calls=%fused_computation.25 | convolution fusion | flops 952369152 | bytes 60817412 | tf_op jit(solution)/shard_map/mdr,mdc->rmc/dot_general | solution.py:60
  757.6 126.8 %reduce-scatter.2.cloned.1.call-done = f32[128,1,3584]{0,2,1:T(8,128)} async-done(((f32[512,1,3584]{0,2,1:T(8,128)}), f32[128,1,3584]{0,2,1:T(8,128)}) %reduce-scatter.2.cloned.1.call-update) | async-done | bytes 1835024 | tf_op jit(solution)/shard_map/reduce_scatter | solution.py:70
  884.4 1.6 convert_element_type.67
  (72 shorter events, 20.4 us)
Async XLA Ops:
  143.5 167.7 %all-to-all-start = ((bf16[8,2,458752]{2,1,0:T(2,128)(2,1)}), bf16[8,2,458752]{2,1,0:T(2,128)(2,1)}, u32[]{:S(2)}, u32[]{:S(2)}) async-start(bf16[8,2,458752]{2,1,0:T(2,128)(2,1)} %reshape.534), calls=%async_computation | async-start | bytes 29360128 | tf_op jit(solution)/shard_map/all_to_all | solution.py:28
  149.0 396.3 %all-reduce.3.cloned.1.call-start = ((), (), s32[]{:S(2)}) async-start(), calls=%async_computation.2 | async-start | bytes 2097152 | tf_op jit(solution)/shard_map/psum | solution.py:47
  414.4 470.0 %reduce-scatter.2.cloned.1.call-start = ((), (), s32[]{:S(2)}) async-start(), calls=%async_computation.3 | async-start | bytes 9175040 | tf_op jit(solution)/shard_map/reduce_scatter | solution.py:70
  632.0 70.9 %slice-start = ((s8[14680064]{0:T(1024)(128)(4,1)}), s8[2097152]{0:T(1024)(128)(4,1)S(1)}, s32[]{:S(2)}) async-start(s8[14680064]{0:T(1024)(128)(4,1)} %bitcast.247), calls=%async_computation.4 | async-start | bytes 4194304
  689.4 6.7 collective-permute-start
  689.5 13.4 %slice-start.1 = ((s8[14680064]{0:T(1024)(128)(4,1)}), s8[4194304]{0:T(1024)(128)(4,1)S(1)}, s32[]{:S(2)}) async-start(s8[14680064]{0:T(1024)(128)(4,1)} %bitcast.247), calls=%async_computation.5 | async-start | bytes 8388608
  689.5 13.4 %slice-start.2 = ((s8[14680064]{0:T(1024)(128)(4,1)}), s8[4194304]{0:T(1024)(128)(4,1)S(1)}, s32[]{:S(2)}) async-start(s8[14680064]{0:T(1024)(128)(4,1)} %bitcast.247), calls=%async_computation.6 | async-start | bytes 8388608
  695.3 7.6 slice-start.3
  696.1 6.7 collective-permute-start.1
  702.8 6.7 collective-permute-start.2
  709.5 6.7 collective-permute-start.3
  716.2 6.7 collective-permute-start.4
  722.9 6.9 collective-permute-start.5
  729.8 6.7 collective-permute-start.6
Sparse Core Ops, SparseCore 0:
  414.5 130.8 all-reduce.2
  757.7 126.6 reduce-scatter.1
